TPU v7x, 32 devices: a whole 2x2x4 slice. The times are simulated.
32 devices in a mesh: task: 2 (over y), row: 4 (over z), col: 4 (over x, core).
Axes of the slice: x: 2, y: 2, z: 4, core: 2. Of those that a mesh axis runs over, the one named last changes fastest.
Arguments:
- features: bfloat16 [164, 4096], P(None, ('task', 'row', 'col')), parts along dimension 1, may hold values from -6 to 6
- rung_index: int32 [4096], P(('task', 'row', 'col')), parts along dimension 0, may hold values from 0 to 3
- w_first: bfloat16 [164, 512], replicated, may hold values from -0.5 to 0.5
- b_first: float32 [512], replicated, may hold values from -4 to 4
- w_second: bfloat16 [512, 512], replicated, may hold values from -0.25 to 0.25
- b_second: float32 [512], replicated, may hold values from -4 to 4
- w_third: bfloat16 [512, 64], replicated, may hold values from -0.25 to 0.25
- targets: float32 [16, 4096], P(None, ('task', 'row', 'col')), parts along dimension 1, may hold values from -80 to 80
- fidelity_factor: float32 [8, 4], P('task'), parts along dimension 0, may hold values from -4 to 4
- inverse_scale: float32 [2], P('task'), parts along dimension 0, may hold values from 0.02 to 0.1
- noise_var: float32 [2], P('task'), parts along dimension 0, may hold values from 0.3 to 1
Outputs:
- solution: float32 [16, 4096], P(None, ('task', 'row', 'col')), parts along dimension 1
- residual: float32 [16, 4096], P(None, ('task', 'row', 'col')), parts along dimension 1
There are 2 independent parts, one for each index of `task`. A program takes and returns all parts, laid end to end along the dimension named above; an argument that names none is the same for every part. Nothing has to cross between parts.
All inputs are finite; a program needn't handle non-finite values.
Results may differ from a plain program's by a relative error of at most 0.012.
The roundings to bfloat16 on the way count: a program that leaves them out, or rounds other values in their place, can miss the bound.
Values may be sent and summed in bfloat16 or wider, within the bound.
No kernel may reach another device: no remote copies, remote signals or barrier semaphores. Data moves between devices by JAX's collectives and lax.ppermute only.
A program may use at most 64 MiB of HBM per device.

v0:
```python
import jax
import jax.numpy as jnp
from jax import lax
from jax.sharding import PartitionSpec as P

ITERS = 2


def fidelity_matrix(fidelity_factor):
    lower = jnp.tril(fidelity_factor)
    return jnp.dot(lower, lower.T, precision=lax.Precision.HIGHEST) + 0.5 * jnp.eye(
        fidelity_factor.shape[0], dtype=jnp.float32
    )


def left_product(weights, values):
    return lax.dot_general(
        weights, values, (((0,), (0,)), ((), ())), preferred_element_type=jnp.float32
    )


def outer_gram(left_side, right_side):
    return lax.dot_general(
        left_side, right_side, (((1,), (1,)), ((), ())), precision=lax.Precision.HIGHEST
    )


def solve_spd(matrix, right_side):
    return jax.scipy.linalg.cho_solve((jnp.linalg.cholesky(matrix), True), right_side)


def block_size(total_count, largest):
    chosen = min(total_count, largest)
    while total_count % chosen != 0:
        chosen = chosen - 1
    return chosen


def rung_fidelity(fidelity, rung_value):
    levels = jnp.arange(fidelity.shape[0], dtype=jnp.float32)
    onehot = (rung_value.astype(jnp.float32)[None, :] == levels[:, None]).astype(jnp.float32)
    return jnp.dot(fidelity, onehot, precision=lax.Precision.HIGHEST)


def kernel_image(embedding, squares, rung_value, col_fidelity, inverse_scale, direction):
    count = embedding.shape[1]
    row_block = block_size(count, 2048)
    col_block = block_size(count, 2048)
    levels = jnp.arange(col_fidelity.shape[0], dtype=jnp.float32)

    def one_row_block(block_number):
        first_row = block_number * row_block
        rows_embedding = lax.dynamic_slice_in_dim(embedding, first_row, row_block, 1)
        rows_squares = lax.dynamic_slice_in_dim(squares, first_row, row_block, 0)
        rows_rung = lax.dynamic_slice_in_dim(rung_value, first_row, row_block, 0)
        rows_match = rows_rung.astype(jnp.float32)[:, None] == levels[None, :]

        def one_col_block(running, column_number):
            first_col = column_number * col_block
            cols_embedding = lax.dynamic_slice_in_dim(embedding, first_col, col_block, 1)
            cols_squares = lax.dynamic_slice_in_dim(squares, first_col, col_block, 0)
            cols_fidelity = lax.dynamic_slice_in_dim(col_fidelity, first_col, col_block, 1)
            cols_direction = lax.dynamic_slice_in_dim(direction, first_col, col_block, 1)
            inner = left_product(rows_embedding, cols_embedding)
            distance = rows_squares[:, None] + cols_squares[None, :] - 2.0 * inner
            tile_fidelity = cols_fidelity[0][None, :]
            for level in range(1, col_fidelity.shape[0]):
                tile_fidelity = jnp.where(
                    rows_match[:, level : level + 1], cols_fidelity[level][None, :], tile_fidelity
                )
            kernel = jnp.exp(-inverse_scale[0] * distance) * tile_fidelity
            contribution = lax.dot_general(
                cols_direction, kernel, (((1,), (1,)), ((), ())), precision=lax.Precision.HIGHEST
            )
            return (running + contribution, None)

        start_value = jnp.zeros((direction.shape[0], row_block), jnp.float32)
        result, unused = lax.scan(
            one_col_block, start_value, jnp.arange(count // col_block, dtype=jnp.int32)
        )
        return result

    stacked = lax.map(one_row_block, jnp.arange(count // row_block, dtype=jnp.int32))
    return jnp.transpose(stacked, (1, 0, 2)).reshape(direction.shape[0], count)


def on_device(
    features,
    rung_index,
    w_first,
    b_first,
    w_second,
    b_second,
    w_third,
    targets,
    fidelity_factor,
    inverse_scale,
    noise_var,
):
    fidelity = fidelity_matrix(fidelity_factor)
    hidden_one = jax.nn.silu(left_product(w_first, features) + b_first[:, None]).astype(
        jnp.bfloat16
    )
    hidden_two = jax.nn.silu(left_product(w_second, hidden_one) + b_second[:, None]).astype(
        jnp.bfloat16
    )
    embedding = left_product(w_third, hidden_two).astype(jnp.bfloat16)
    rung_value = rung_index.astype(jnp.float32).astype(jnp.bfloat16)
    own_count = targets.shape[1]
    own_first = (lax.axis_index("row") * lax.axis_size("col") + lax.axis_index("col")) * own_count
    all_embedding = lax.all_gather(embedding, ("row", "col"), axis=1, tiled=True)
    all_rung = lax.all_gather(rung_value, ("row", "col"), axis=0, tiled=True)
    all_targets = lax.all_gather(targets, ("row", "col"), axis=1, tiled=True)
    squares = jnp.sum(jnp.square(all_embedding.astype(jnp.float32)), axis=0)
    col_fidelity = rung_fidelity(fidelity, all_rung)
    solution = jnp.zeros_like(all_targets)
    residual = all_targets
    direction = all_targets
    gram = outer_gram(residual, residual)
    for iteration in range(ITERS):
        image = (
            kernel_image(all_embedding, squares, all_rung, col_fidelity, inverse_scale, direction)
            + noise_var[0] * direction
        )
        curvature = outer_gram(direction, image)
        step_matrix = solve_spd(curvature, gram)
        solution = solution + jnp.dot(step_matrix.T, direction, precision=lax.Precision.HIGHEST)
        residual = residual - jnp.dot(step_matrix.T, image, precision=lax.Precision.HIGHEST)
        if iteration + 1 < ITERS:
            new_gram = outer_gram(residual, residual)
            update_matrix = solve_spd(gram, new_gram)
            direction = residual + jnp.dot(
                update_matrix.T, direction, precision=lax.Precision.HIGHEST
            )
            gram = new_gram
    own_solution = lax.dynamic_slice_in_dim(solution, own_first, own_count, 1)
    own_residual = lax.dynamic_slice_in_dim(residual, own_first, own_count, 1)
    return (own_solution, own_residual)


def solution(mesh):
    placed = (
        P(None, ("task", "row", "col")),
        P(("task", "row", "col")),
        P(),
        P(),
        P(),
        P(),
        P(),
        P(None, ("task", "row", "col")),
        P("task", None),
        P("task"),
        P("task"),
    )
    return jax.shard_map(
        on_device,
        mesh=mesh,
        in_specs=placed,
        out_specs=(P(None, ("task", "row", "col")), P(None, ("task", "row", "col"))),
        check_vma=False,
    )
```

profile of v0, /device:TPU:0, one launch (start us, length us, event | category | flops | bytes accessed | tf_op | source)
XLA Modules:
  0.0 122.0 jit_solution(9418712131245514869)
XLA Ops:
  0.6 0.7 convert_bitcast_fusion
  1.4 23.1 %all-gather = bf16[16,1,128]{2,1,0:T(2,128)(2,1)S(1)} all-gather(bf16[1,1,128]{2,1,0:T(2,128)(2,1)S(1)} %convert_bitcast_fusion), channel_id=1, replica_groups=mesh['task'=2,'row'=4,'col'=4] {'row','col'}, dimensions={0}, use_global_device_ids=true | all-gather | bytes 4352 | tf_op jit(solution)/shard_map/all_gather | solution.py:112
  24.5 0.9 convolution_add_fusion.4
  25.7 1.3 %multiply_convert_fusion.1 = bf16[512,128]{1,0:T(8,128)(2,1)S(1)} fusion(bf16[164,512]{1,0:T(8,128)(2,1)} %param.16, bf16[164,128]{1,0:T(8,128)(2,1)} %param.14, f32[512]{0:T(512)} %param.17), kind=kOutput, calls=%fused_computation.14 | convolution fusion | flops 21889024 | bytes 343040 | tf_op jit(solution)/shard_map/dot_general | solution.py:17
  26.9 1.4 %fusion.2 = bf16[64,128]{1,0:T(8,128)(2,1)S(1)} fusion(bf16[512,64]{0,1:T(8,128)(2,1)} %param.20, bf16[512,128]{1,0:T(8,128)(2,1)S(1)} %multiply_convert_fusion.1, bf16[512,512]{1,0:T(8,128)(2,1)S(1)} %copy-done, f32[512]{0:T(512)} %param.19), kind=kOutput, calls=%fused_computation.10 | convolution fusion | flops 75898880 | bytes 739328 | tf_op jit(solution)/shard_map/dot_general | solution.py:17
  28.3 18.2 %all_gather.9 = bf16[64,2048]{1,0:T(8,128)(2,1)S(1)} all-gather(bf16[64,128]{1,0:T(8,128)(2,1)S(1)} %fusion.2), channel_id=1, replica_groups=mesh['task'=2,'row'=4,'col'=4] {'row','col'}, dimensions={1}, use_global_device_ids=true | all-gather | bytes 278528 | tf_op jit(solution)/shard_map/all_gather | solution.py:111
  47.2 6.6 %select_multiply_fusion = f32[2048,2048]{1,0:T(8,128)S(1)} fusion(bf16[64,2048]{1,0:T(8,128)(2,1)S(1)} %all_gather.9, f32[2048]{0:T(1024)S(1)} %bitcast.95, f32[2048]{0:T(1024)S(1)} %bitcast.96, f32[2048]{0:T(1024)S(1)} %bitcast.97, f32[2048]{0:T(1024)S(1)} %bitcast.94, f32[2048]{0:T(1024)S(1)} %multiply_reduce_fusion, f32[]{:T(128)} %bitcast, ...), kind=kOutput, calls=%fused_computation | convolution fusion | flops 570425344 | bytes 17086468 | tf_op jit(solution)/shard_map/while/body/eval_jaxpr/while/body/eval_jaxpr/dot_general | solution.py:17
  53.8 19.3 %all_gather.11 = f32[16,2048]{1,0:T(8,128)S(1)} all-gather(f32[16,128]{1,0:T(8,128)S(1)} %copy-done.2), channel_id=1, replica_groups=mesh['task'=2,'row'=4,'col'=4] {'row','col'}, dimensions={1}, use_global_device_ids=true | all-gather | bytes 139264 | tf_op jit(solution)/shard_map/all_gather | solution.py:113
  73.8 14.1 %fusion = f32[16,2048]{1,0:T(8,128)S(1)} fusion(f32[2048,2048]{1,0:T(8,128)S(1)} %select_multiply_fusion, f32[16,2048]{1,0:T(8,128)S(1)} %all_gather.11, f32[]{:T(128)} %bitcast.89), kind=kOutput, calls=%fused_computation.5 | convolution fusion | flops 805371904 | bytes 17039364 | tf_op jit(solution)/shard_map/while/body/eval_jaxpr/while/body/eval_jaxpr/dot_general | solution.py:72
  88.2 1.5 %cholesky.59 = f32[16,16]{1,0:T(8,128)S(1)} custom-call(f32[16,16]{1,0:T(8,128)S(1)} %add_multiply_fusion), custom_call_target="Cholesky" | custom-call | tf_op jit(solution)/shard_map/jit(cholesky)/cholesky | solution.py:29
  89.8 0.6 compare_reduce_fusion.2
  90.4 0.6 fusion.7
  91.1 1.2 %custom-call.9 = f32[1,16,16]{1,2,0:T(8,128)S(1)} custom-call(f32[1,16,16]{2,1,0:T(8,128)S(1)} %fusion.7), custom_call_target="InvertDiagBlocksLowerTriangular" | custom-call | tf_op jit(solution)/shard_map/jit(_cho_solve)/triangular_solve | solution.py:29
  93.3 0.4 fusion.32
  93.8 1.5 %cholesky.70 = f32[16,16]{1,0:T(8,128)S(1)} custom-call(f32[16,16]{1,0:T(8,128)S(1)} %fusion.19), custom_call_target="Cholesky" | custom-call | tf_op jit(solution)/shard_map/jit(cholesky)/cholesky | solution.py:29
  95.4 0.6 compare_reduce_fusion.1
  96.0 0.6 fusion.8
  96.7 1.2 %custom-call.10 = f32[1,16,16]{1,2,0:T(8,128)S(1)} custom-call(f32[1,16,16]{2,1,0:T(8,128)S(1)} %fusion.8), custom_call_target="InvertDiagBlocksLowerTriangular" | custom-call | tf_op jit(solution)/shard_map/jit(_cho_solve)/triangular_solve | solution.py:29
  98.6 17.1 %convolution_add_fusion.1 = f32[16,2048]{1,0:T(8,128)S(1)} fusion(f32[16,2048]{1,0:T(8,128)S(1)} %convolution_add_fusion, f32[2048,2048]{1,0:T(8,128)} %copy-done.1, f32[]{:T(128)} %bitcast.90), kind=kOutput, calls=%fused_computation.3 | convolution fusion | flops 805371904 | bytes 17039364 | tf_op jit(solution)/shard_map/while/body/eval_jaxpr/while/body/eval_jaxpr/dot_general | solution.py:72
  116.0 1.5 %cholesky.81 = f32[16,16]{1,0:T(8,128)S(1)} custom-call(f32[16,16]{1,0:T(8,128)S(1)} %fusion.14), custom_call_target="Cholesky" | custom-call | tf_op jit(solution)/shard_map/jit(cholesky)/cholesky | solution.py:29
  117.5 0.6 compare_reduce_fusion
  118.2 0.6 fusion.9
  118.9 1.2 %custom-call.11 = f32[1,16,16]{1,2,0:T(8,128)S(1)} custom-call(f32[1,16,16]{2,1,0:T(8,128)S(1)} %fusion.9), custom_call_target="InvertDiagBlocksLowerTriangular" | custom-call | tf_op jit(solution)/shard_map/jit(_cho_solve)/triangular_solve | solution.py:29
  121.4 0.6 dynamic-slice_subtract_fusion
  (35 shorter events, 4.2 us)
Async XLA Ops:
  0.6 26.3 %copy-start = (bf16[512,512]{1,0:T(8,128)(2,1)S(1)}, bf16[512,512]{1,0:T(8,128)(2,1)}, u32[]{:S(2)}) copy-start(bf16[512,512]{1,0:T(8,128)(2,1)} %param.18) | copy-start | bytes 1572868
  47.2 6.6 %copy-start.2 = (f32[16,128]{1,0:T(8,128)S(1)}, f32[16,128]{1,0:T(8,128)}, u32[]{:S(2)}) copy-start(f32[16,128]{1,0:T(8,128)} %param.21) | copy-start | bytes 24580
  53.8 20.0 %copy-start.1 = (f32[2048,2048]{1,0:T(8,128)}, f32[2048,2048]{1,0:T(8,128)S(1)}, u32[]{:S(2)}) copy-start(f32[2048,2048]{1,0:T(8,128)S(1)} %select_multiply_fusion) | copy-start | bytes 50331652
where the time goes:
time: 122 us
  blocking collectives  60.5 us (50%)
  matrix products  45.3 us (37%)
  other arithmetic  13.7 us (11%)
  between operations  2.14 us (2%)
    dot_general x2, matrix products, one_col_block(): lax.dot_general(cols_direction, kernel, (((1,), (1,)), ((), ())), precisi...  31.2 us
    all_gather x1, blocking collectives, on_device(): all_rung = lax.all_gather(rung_value, ('row', 'col'), axis=0, tiled=True)  23.1 us
    all_gather x1, blocking collectives, on_device(): all_targets = lax.all_gather(targets, ('row', 'col'), axis=1, tiled=True)  19.3 us
    all_gather x1, blocking collectives, on_device(): lax.all_gather(embedding, ('row', 'col'), axis=1, tiled=True)  18.2 us
    dot_general x3, matrix products, left_product(): lax.dot_general(weights, values, (((0,), (0,)), ((), ())), preferred_elem...  9.19 us
    another operation x9, other arithmetic, solve_spd(): jnp.linalg.cholesky(matrix)  6.57 us
    another operation x6, other arithmetic, solve_spd(): jax.scipy.linalg.cho_solve((jnp.linalg.cholesky(matrix), True), right_side)  5.63 us

commit v1 on v0

--- a/solution.py
+++ b/solution.py
@@ -110,7 +110,26 @@
     own_first = (lax.axis_index("row") * lax.axis_size("col") + lax.axis_index("col")) * own_count
     all_embedding = lax.all_gather(embedding, ("row", "col"), axis=1, tiled=True)
     all_rung = lax.all_gather(rung_value, ("row", "col"), axis=0, tiled=True)
-    all_targets = lax.all_gather(targets, ("row", "col"), axis=1, tiled=True)
+    size, index, width = (
+        lax.axis_size(("row", "col")),
+        lax.axis_index(("row", "col")),
+        targets.shape[1],
+    )
+    ahead = [(i, (i + 1) % size) for i in range(size)]
+    downward = [(i, (i - 1) % size) for i in range(size)]
+    out = jnp.zeros((*targets.shape[:1], size * width, *targets.shape[1 + 1 :]), targets.dtype)
+    out = lax.dynamic_update_slice_in_dim(out, targets, index * width, axis=1)
+    from_left = from_right = targets
+    middle = size // 2
+    for turn in range(1, middle + 1):
+        from_left = lax.ppermute(from_left, ("row", "col"), ahead)
+        out = lax.dynamic_update_slice_in_dim(out, from_left, (index - turn) % size * width, axis=1)
+        if turn < size - middle:
+            from_right = lax.ppermute(from_right, ("row", "col"), downward)
+            out = lax.dynamic_update_slice_in_dim(
+                out, from_right, (index + turn) % size * width, axis=1
+            )
+    all_targets = out
     squares = jnp.sum(jnp.square(all_embedding.astype(jnp.float32)), axis=0)
     col_fidelity = rung_fidelity(fidelity, all_rung)
     solution = jnp.zeros_like(all_targets)

time: 122 us -> 153 us (1.25)
  starting transfers between devices: 0 us -> 28.5 us
  blocking collectives: 60.5 us -> 37 us
  waiting for transfers between devices: 0 us -> 18.4 us
  matrix products: 45.3 us -> 52.2 us
    ppermute x0 -> x15, starting transfers between devices: none -> 28.5 us  [the longest x7 28.5 us: on_device(): from_right = lax.ppermute(from_right, ('row', 'col'), downward)]
    all_gather x1 -> x0, blocking collectives: 19.3 us -> none  [on_device(): all_targets = lax.all_gather(targets, ('row', 'col'), axis=1, tiled=True)]
    ppermute x0 -> x15, waiting for transfers between devices: none -> 18.4 us  [the longest x8 11.8 us: on_device(): from_left = lax.ppermute(from_left, ('row', 'col'), ahead)]
    all_gather x1, blocking collectives: 23.1 us -> 18.2 us  [on_device(): all_rung = lax.all_gather(rung_value, ('row', 'col'), axis=0, tiled=True)]
    dot_general x3, matrix products: 9.19 us -> 13.1 us  [left_product(): lax.dot_general(weights, values, (((0,), (0,)), ((), ())), preferred_elem...]
    dot_general x2, matrix products: 31.2 us -> 34.4 us  [one_col_block(): lax.dot_general(cols_direction, kernel, (((1,), (1,)), ((), ())), precisi...]
  transfers between devices with their start and end apart: 0 -> 15, of which waited for: 0 -> 12; matrix products, arithmetic and copies ran while one was open for 0% -> 10% of each run, Pallas kernels for 0% -> 0%
where the time goes in v1:
time: 153 us
  matrix products  52.2 us (34%)
  blocking collectives  37 us (24%)
  starting transfers between devices  28.5 us (19%)
  waiting for transfers between devices  18.4 us (12%)
  other arithmetic  13.5 us (9%)
  between operations  2.2 us (1%)
    dot_general x2, matrix products, one_col_block(): lax.dot_general(cols_direction, kernel, (((1,), (1,)), ((), ())), precisi...  34.4 us
    ppermute x7, starting transfers between devices, on_device(): from_right = lax.ppermute(from_right, ('row', 'col'), downward)  28.5 us
    all_gather x1, blocking collectives, on_device(): lax.all_gather(embedding, ('row', 'col'), axis=1, tiled=True)  18.9 us
    all_gather x1, blocking collectives, on_device(): all_rung = lax.all_gather(rung_value, ('row', 'col'), axis=0, tiled=True)  18.2 us
    dot_general x3, matrix products, left_product(): lax.dot_general(weights, values, (((0,), (0,)), ((), ())), preferred_elem...  13.1 us
    ppermute x8, waiting for transfers between devices, on_device(): from_left = lax.ppermute(from_left, ('row', 'col'), ahead)  11.8 us
    ppermute x7, waiting for transfers between devices, on_device(): from_right = lax.ppermute(from_right, ('row', 'col'), downward)  6.52 us
    another operation x9, other arithmetic, solve_spd(): jnp.linalg.cholesky(matrix)  6.51 us
  transfers between devices with their start and end apart: 15, of which 12 were waited for; matrix products, arithmetic and copies ran while one was open for 10% of the time, Pallas kernels for 0%

profile of v1, /device:TPU:0, one launch (start us, length us, event | category | flops | bytes accessed | tf_op | source)
XLA Modules:
  0.0 153.0 jit_solution(3476453525820292596)
XLA Ops:
  0.6 5.5 %collective-permute-start.1 = (f32[16,128]{1,0:T(8,128)}, f32[16,128]{1,0:T(8,128)S(1)}, u32[]{:S(2)}, u32[]{:S(2)}) collective-permute-start(f32[16,128]{1,0:T(8,128)} %param.21), channel_id=1, source_target_pairs={{0,15},{1,0},{2,1},{3,2},{4,3},{5,4},{6,5},{7,6},{8,7},{9,8},{10,9... | collective-permute-start | bytes 24584 | tf_op jit(solution)/shard_map/ppermute | solution.py:128
  8.3 18.2 %all-gather = bf16[16,1,128]{2,1,0:T(2,128)(2,1)S(1)} all-gather(bf16[1,1,128]{2,1,0:T(2,128)(2,1)S(1)} %convert_bitcast_fusion), channel_id=1, replica_groups=mesh['task'=2,'row'=4,'col'=4] {'row','col'}, dimensions={0}, use_global_device_ids=true | all-gather | bytes 4352 | tf_op jit(solution)/shard_map/all_gather | solution.py:112
  26.8 1.3 multiply_convert_fusion.1
  28.1 1.3 fusion.1
  29.4 18.9 %all_gather.6 = bf16[64,2048]{1,0:T(8,128)(2,1)S(1)} all-gather(bf16[64,128]{1,0:T(8,128)(2,1)S(1)} %fusion.1), channel_id=1, replica_groups=mesh['task'=2,'row'=4,'col'=4] {'row','col'}, dimensions={1}, use_global_device_ids=true | all-gather | bytes 278528 | tf_op jit(solution)/shard_map/all_gather | solution.py:111
  49.1 10.5 %select_multiply_fusion = f32[2048,2048]{1,0:T(8,128)} fusion(bf16[64,2048]{1,0:T(8,128)(2,1)S(1)} %all_gather.6, f32[2048]{0:T(1024)S(1)} %bitcast.90, f32[2048]{0:T(1024)S(1)} %bitcast.91, f32[2048]{0:T(1024)S(1)} %bitcast.92, f32[2048]{0:T(1024)S(1)} %bitcast.89, f32[2048]{0:T(1024)S(1)} %multiply_reduce_fusion, f32[]{:T(128)} %bitcast, ...), kind=kOutput, calls=%fused_computation | convolution fusion | flops 570425344 | bytes 17086468 | tf_op jit(solution)/shard_map/while/body/eval_jaxpr/while/body/eval_jaxpr/dot_general | solution.py:17
  61.3 1.3 collective-permute-done.3
  62.7 4.4 %collective-permute-start.5 = (f32[16,128]{1,0:T(8,128)S(1)}, f32[16,128]{1,0:T(8,128)S(1)}, u32[]{:S(2)}, u32[]{:S(2)}) collective-permute-start(f32[16,128]{1,0:T(8,128)S(1)} %collective-permute-done.3), channel_id=1, source_target_pairs={{0,15},{1,0},{2,1},{3,2},{4,3},{5,4},{6,5},{7,6},{8,7},{9,8},{10,9... | collective-permute-start | bytes 24584 | tf_op jit(solution)/shard_map/ppermute | solution.py:128
  67.2 1.3 collective-permute-done.5
  68.5 4.4 %collective-permute-start.7 = (f32[16,128]{1,0:T(8,128)S(1)}, f32[16,128]{1,0:T(8,128)S(1)}, u32[]{:S(2)}, u32[]{:S(2)}) collective-permute-start(f32[16,128]{1,0:T(8,128)S(1)} %collective-permute-done.5), channel_id=1, source_target_pairs={{0,15},{1,0},{2,1},{3,2},{4,3},{5,4},{6,5},{7,6},{8,7},{9,8},{10,9... | collective-permute-start | bytes 24584 | tf_op jit(solution)/shard_map/ppermute | solution.py:128
  72.9 1.3 collective-permute-done.7
  74.2 4.4 %collective-permute-start.9 = (f32[16,128]{1,0:T(8,128)S(1)}, f32[16,128]{1,0:T(8,128)S(1)}, u32[]{:S(2)}, u32[]{:S(2)}) collective-permute-start(f32[16,128]{1,0:T(8,128)S(1)} %collective-permute-done.7), channel_id=1, source_target_pairs={{0,15},{1,0},{2,1},{3,2},{4,3},{5,4},{6,5},{7,6},{8,7},{9,8},{10,9... | collective-permute-start | bytes 24584 | tf_op jit(solution)/shard_map/ppermute | solution.py:128
  78.7 1.3 collective-permute-done.9
  80.0 4.4 %collective-permute-start.11 = (f32[16,128]{1,0:T(8,128)S(1)}, f32[16,128]{1,0:T(8,128)S(1)}, u32[]{:S(2)}, u32[]{:S(2)}) collective-permute-start(f32[16,128]{1,0:T(8,128)S(1)} %collective-permute-done.9), channel_id=1, source_target_pairs={{0,15},{1,0},{2,1},{3,2},{4,3},{5,4},{6,5},{7,6},{8,7},{9,8},{10,9... | collective-permute-start | bytes 24584 | tf_op jit(solution)/shard_map/ppermute | solution.py:128
  84.5 1.3 collective-permute-done.11
  85.8 4.4 %collective-permute-start.13 = (f32[16,128]{1,0:T(8,128)S(1)}, f32[16,128]{1,0:T(8,128)S(1)}, u32[]{:S(2)}, u32[]{:S(2)}) collective-permute-start(f32[16,128]{1,0:T(8,128)S(1)} %collective-permute-done.11), channel_id=1, source_target_pairs={{0,15},{1,0},{2,1},{3,2},{4,3},{5,4},{6,5},{7,6},{8,7},{9,8},{10,9... | collective-permute-start | bytes 24584 | tf_op jit(solution)/shard_map/ppermute | solution.py:128
  90.3 5.8 %collective-permute-done.12 = f32[16,128]{1,0:T(8,128)S(1)} collective-permute-done((f32[16,128]{1,0:T(8,128)S(1)}, f32[16,128]{1,0:T(8,128)S(1)}, u32[]{:S(2)}, u32[]{:S(2)}) %collective-permute-start.12) | collective-permute-done | bytes 8224 | tf_op jit(solution)/shard_map/ppermute | solution.py:125
  96.1 5.7 %collective-permute-done.14 = f32[16,128]{1,0:T(8,128)S(1)} collective-permute-done((f32[16,128]{1,0:T(8,128)S(1)}, f32[16,128]{1,0:T(8,128)S(1)}, u32[]{:S(2)}, u32[]{:S(2)}) %collective-permute-start.14) | collective-permute-done | bytes 8224 | tf_op jit(solution)/shard_map/ppermute | solution.py:125
  102.1 17.1 %convolution_add_fusion.1 = f32[16,2048]{1,0:T(8,128)S(1)} fusion(f32[16,2048]{1,0:T(8,128)S(1)} %constant_dynamic-update-slice_fusion, f32[2048,2048]{1,0:T(8,128)} %select_multiply_fusion, f32[]{:T(128)} %bitcast.84), kind=kOutput, calls=%fused_computation.3 | convolution fusion | flops 805371904 | bytes 17039364 | tf_op jit(solution)/shard_map/while/body/eval_jaxpr/while/body/eval_jaxpr/dot_general | solution.py:72
  119.6 1.5 cholesky.59
  122.4 1.2 custom-call.9
  124.7 1.4 cholesky.70
  129.7 17.3 %fusion.37 = f32[16,2048]{1,0:T(8,128)S(1)} fusion(f32[16,2048]{1,0:T(8,128)S(1)} %convolution_add_fusion, f32[2048,2048]{1,0:T(8,128)} %select_multiply_fusion), kind=kOutput, calls=%fused_computation.89 | convolution fusion | flops 805306368 | bytes 17039360 | tf_op jit(solution)/shard_map/while/body/eval_jaxpr/while/body/eval_jaxpr/dot_general | solution.py:72
  147.3 1.5 cholesky.81
  (77 shorter events, 15.0 us)
Async XLA Ops:
  0.6 27.5 %copy-start = (bf16[512,512]{1,0:T(8,128)(2,1)S(1)}, bf16[512,512]{1,0:T(8,128)(2,1)}, u32[]{:S(2)}) copy-start(bf16[512,512]{1,0:T(8,128)(2,1)} %param.18) | copy-start | bytes 1572868
  0.6 59.7 %collective-permute-start.1 = (f32[16,128]{1,0:T(8,128)}, f32[16,128]{1,0:T(8,128)S(1)}, u32[]{:S(2)}, u32[]{:S(2)}) collective-permute-start(f32[16,128]{1,0:T(8,128)} %param.21), channel_id=1, source_target_pairs={{0,15},{1,0},{2,1},{3,2},{4,3},{5,4},{6,5},{7,6},{8,7},{9,8},{10,9... | collective-permute-start | bytes 24584 | tf_op jit(solution)/shard_map/ppermute | solution.py:128
  6.1 55.2 %collective-permute-start = (f32[16,128]{1,0:T(8,128)}, f32[16,128]{1,0:T(8,128)S(1)}, u32[]{:S(2)}, u32[]{:S(2)}) collective-permute-start(f32[16,128]{1,0:T(8,128)} %param.21), channel_id=1, source_target_pairs={{0,1},{1,2},{2,3},{3,4},{4,5},{5,6},{6,7},{7,8},{8,9},{9,10},{10,1... | collective-permute-start | bytes 24584 | tf_op jit(solution)/shard_map/ppermute | solution.py:125
  60.4 2.3 %collective-permute-start.3 = (f32[16,128]{1,0:T(8,128)S(1)}, f32[16,128]{1,0:T(8,128)S(1)}, u32[]{:S(2)}, u32[]{:S(2)}) collective-permute-start(f32[16,128]{1,0:T(8,128)S(1)} %collective-permute-done.1), channel_id=1, source_target_pairs={{0,15},{1,0},{2,1},{3,2},{4,3},{5,4},{6,5},{7,6},{8,7},{9,8},{10,9... | collective-permute-start | bytes 24584 | tf_op jit(solution)/shard_map/ppermute | solution.py:128
  61.3 5.9 %collective-permute-start.2 = (f32[16,128]{1,0:T(8,128)S(1)}, f32[16,128]{1,0:T(8,128)S(1)}, u32[]{:S(2)}, u32[]{:S(2)}) collective-permute-start(f32[16,128]{1,0:T(8,128)S(1)} %collective-permute-done), channel_id=1, source_target_pairs={{0,1},{1,2},{2,3},{3,4},{4,5},{5,6},{6,7},{7,8},{8,9},{9,10},{10,1... | collective-permute-start | bytes 24584 | tf_op jit(solution)/shard_map/ppermute | solution.py:125
  62.7 5.8 %collective-permute-start.5 = (f32[16,128]{1,0:T(8,128)S(1)}, f32[16,128]{1,0:T(8,128)S(1)}, u32[]{:S(2)}, u32[]{:S(2)}) collective-permute-start(f32[16,128]{1,0:T(8,128)S(1)} %collective-permute-done.3), channel_id=1, source_target_pairs={{0,15},{1,0},{2,1},{3,2},{4,3},{5,4},{6,5},{7,6},{8,7},{9,8},{10,9... | collective-permute-start | bytes 24584 | tf_op jit(solution)/shard_map/ppermute | solution.py:128
  67.2 5.8 %collective-permute-start.4 = (f32[16,128]{1,0:T(8,128)S(1)}, f32[16,128]{1,0:T(8,128)S(1)}, u32[]{:S(2)}, u32[]{:S(2)}) collective-permute-start(f32[16,128]{1,0:T(8,128)S(1)} %collective-permute-done.2), channel_id=1, source_target_pairs={{0,1},{1,2},{2,3},{3,4},{4,5},{5,6},{6,7},{7,8},{8,9},{9,10},{10,1... | collective-permute-start | bytes 24584 | tf_op jit(solution)/shard_map/ppermute | solution.py:125
  68.5 5.8 %collective-permute-start.7 = (f32[16,128]{1,0:T(8,128)S(1)}, f32[16,128]{1,0:T(8,128)S(1)}, u32[]{:S(2)}, u32[]{:S(2)}) collective-permute-start(f32[16,128]{1,0:T(8,128)S(1)} %collective-permute-done.5), channel_id=1, source_target_pairs={{0,15},{1,0},{2,1},{3,2},{4,3},{5,4},{6,5},{7,6},{8,7},{9,8},{10,9... | collective-permute-start | bytes 24584 | tf_op jit(solution)/shard_map/ppermute | solution.py:128
  72.9 5.8 %collective-permute-start.6 = (f32[16,128]{1,0:T(8,128)S(1)}, f32[16,128]{1,0:T(8,128)S(1)}, u32[]{:S(2)}, u32[]{:S(2)}) collective-permute-start(f32[16,128]{1,0:T(8,128)S(1)} %collective-permute-done.4), channel_id=1, source_target_pairs={{0,1},{1,2},{2,3},{3,4},{4,5},{5,6},{6,7},{7,8},{8,9},{9,10},{10,1... | collective-permute-start | bytes 24584 | tf_op jit(solution)/shard_map/ppermute | solution.py:125
  74.2 5.8 %collective-permute-start.9 = (f32[16,128]{1,0:T(8,128)S(1)}, f32[16,128]{1,0:T(8,128)S(1)}, u32[]{:S(2)}, u32[]{:S(2)}) collective-permute-start(f32[16,128]{1,0:T(8,128)S(1)} %collective-permute-done.7), channel_id=1, source_target_pairs={{0,15},{1,0},{2,1},{3,2},{4,3},{5,4},{6,5},{7,6},{8,7},{9,8},{10,9... | collective-permute-start | bytes 24584 | tf_op jit(solution)/shard_map/ppermute | solution.py:128
  78.7 5.8 %collective-permute-start.8 = (f32[16,128]{1,0:T(8,128)S(1)}, f32[16,128]{1,0:T(8,128)S(1)}, u32[]{:S(2)}, u32[]{:S(2)}) collective-permute-start(f32[16,128]{1,0:T(8,128)S(1)} %collective-permute-done.6), channel_id=1, source_target_pairs={{0,1},{1,2},{2,3},{3,4},{4,5},{5,6},{6,7},{7,8},{8,9},{9,10},{10,1... | collective-permute-start | bytes 24584 | tf_op jit(solution)/shard_map/ppermute | solution.py:125
  80.0 5.8 %collective-permute-start.11 = (f32[16,128]{1,0:T(8,128)S(1)}, f32[16,128]{1,0:T(8,128)S(1)}, u32[]{:S(2)}, u32[]{:S(2)}) collective-permute-start(f32[16,128]{1,0:T(8,128)S(1)} %collective-permute-done.9), channel_id=1, source_target_pairs={{0,15},{1,0},{2,1},{3,2},{4,3},{5,4},{6,5},{7,6},{8,7},{9,8},{10,9... | collective-permute-start | bytes 24584 | tf_op jit(solution)/shard_map/ppermute | solution.py:128
  84.5 5.8 %collective-permute-start.10 = (f32[16,128]{1,0:T(8,128)S(1)}, f32[16,128]{1,0:T(8,128)S(1)}, u32[]{:S(2)}, u32[]{:S(2)}) collective-permute-start(f32[16,128]{1,0:T(8,128)S(1)} %collective-permute-done.8), channel_id=1, source_target_pairs={{0,1},{1,2},{2,3},{3,4},{4,5},{5,6},{6,7},{7,8},{8,9},{9,10},{10,1... | collective-permute-start | bytes 24584 | tf_op jit(solution)/shard_map/ppermute | solution.py:125
  85.8 10.3 %collective-permute-start.13 = (f32[16,128]{1,0:T(8,128)S(1)}, f32[16,128]{1,0:T(8,128)S(1)}, u32[]{:S(2)}, u32[]{:S(2)}) collective-permute-start(f32[16,128]{1,0:T(8,128)S(1)} %collective-permute-done.11), channel_id=1, source_target_pairs={{0,15},{1,0},{2,1},{3,2},{4,3},{5,4},{6,5},{7,6},{8,7},{9,8},{10,9... | collective-permute-start | bytes 24584 | tf_op jit(solution)/shard_map/ppermute | solution.py:128
  90.3 5.8 %collective-permute-start.12 = (f32[16,128]{1,0:T(8,128)S(1)}, f32[16,128]{1,0:T(8,128)S(1)}, u32[]{:S(2)}, u32[]{:S(2)}) collective-permute-start(f32[16,128]{1,0:T(8,128)S(1)} %collective-permute-done.10), channel_id=1, source_target_pairs={{0,1},{1,2},{2,3},{3,4},{4,5},{5,6},{6,7},{7,8},{8,9},{9,10},{10,1... | collective-permute-start | bytes 24584 | tf_op jit(solution)/shard_map/ppermute | solution.py:125
  96.0 5.8 %collective-permute-start.14 = (f32[16,128]{1,0:T(8,128)S(1)}, f32[16,128]{1,0:T(8,128)S(1)}, u32[]{:S(2)}, u32[]{:S(2)}) collective-permute-start(f32[16,128]{1,0:T(8,128)S(1)} %collective-permute-done.12), channel_id=1, source_target_pairs={{0,1},{1,2},{2,3},{3,4},{4,5},{5,6},{6,7},{7,8},{8,9},{9,10},{10,1... | collective-permute-start | bytes 24584 | tf_op jit(solution)/shard_map/ppermute | solution.py:125
